TPU v7x, 128 devices: a whole 4x4x4 slice. The times are simulated.
128 devices in a mesh: strip: 32 (over y, x, core), visit: 4 (over z).
Axes of the slice: x: 4, y: 4, z: 4, core: 2. Of those that a mesh axis runs over, the one named last changes fastest.
Arguments:
- sky_model: float32 [1024, 4096], P('strip'), may hold values from -6 to 6
- exposures: bfloat16 [16, 1024, 4096], P('visit', 'strip'), may hold values from -6 to 6
- warp_mats: bfloat16 [16, 32, 3, 128, 128], P('visit'), may hold values from -0.3125 to 0.3125
- warp_blocks: int32 [16, 32, 3], P('visit'), may hold values from 0 to 31
- psf_cols: float32 [16, 33], P('visit'), may hold values from 0 to 1, as said below
- psf_rows: float32 [16, 33], P('visit'), may hold values from 0 to 1, as said below
- bad_boxes: int32 [16, 32, 4], P('visit'), may hold values from 0 to 4096, as said below
- footprints: int32 [16, 4], P('visit'), may hold values from 0 to 4096, as said below
Outputs:
- estimate: float32 [1024, 4096], P('strip')
Inputs may be any that keep to these rules, and one draw needn't show every extreme that they name: `bad_boxes`: in each rectangle the end row exceeds the first row and the end column exceeds the first column; ends are exclusive. `footprints`: each tile covers at least the middle half of the rows and of the columns; ends are exclusive. `psf_cols`: kernel taps are positive. `psf_rows`: kernel taps are positive.
All inputs are finite; a program needn't handle non-finite values.
Results may differ from a plain program's by a relative error of at most 0.0003.
Values may be sent and summed in bfloat16 or wider, within the bound.
No kernel may reach another device: no remote copies, remote signals or barrier semaphores. Data moves between devices by JAX's collectives and lax.ppermute only.
A program may use at most 128 MiB of HBM per device.

v0:
```python
import jax
import jax.numpy as jnp
from jax import lax
from jax.sharding import PartitionSpec as P

STEPS = 2


precise = lax.Precision.HIGHEST


def pad_axis(image_stack, axis_pos, margin):
    widths = [(0, 0), (0, 0), (0, 0)]
    widths[axis_pos] = (margin, margin)
    return jnp.pad(image_stack, widths)


def taps_along(padded, kernel, axis_pos, length):
    running = None
    for tap_index in range(kernel.shape[1]):
        shifted = lax.slice_in_dim(padded, tap_index, tap_index + length, axis=axis_pos)
        term = kernel[:, tap_index][:, None, None] * shifted
        running = term if running is None else running + term
    return running


def mask_of(row_ids, col_ids, bad_list, footprint):
    row_hits = (
        (row_ids[None, :] >= bad_list[:, 0:1]) & (row_ids[None, :] < bad_list[:, 1:2])
    ).astype(jnp.float32)
    col_hits = (
        (col_ids[None, :] >= bad_list[:, 2:3]) & (col_ids[None, :] < bad_list[:, 3:4])
    ).astype(jnp.float32)
    covered = jnp.dot(row_hits.T, col_hits, preferred_element_type=jnp.float32)
    inside_rows = ((row_ids >= footprint[0]) & (row_ids < footprint[1])).astype(jnp.float32)
    inside_cols = ((col_ids >= footprint[2]) & (col_ids < footprint[3])).astype(jnp.float32)
    return (
        jnp.where(covered > 0.5, 0.0, 1.0).astype(jnp.float32)
        * inside_rows[:, None]
        * inside_cols[None, :]
    )


def local(sky_model, exposures, warp_mats, warp_blocks, psf_cols, psf_rows, bad_boxes, footprints):
    strips = lax.axis_size("strip")
    strip_index = lax.axis_index("strip")
    visit_count = lax.axis_size("visit")
    rows_local = sky_model.shape[0]
    columns = sky_model.shape[1]
    block_count = columns // 128
    visits_here = warp_mats.shape[0]
    margin = psf_cols.shape[1] // 2
    mats_full = warp_mats.astype(jnp.float32)
    onehot = (warp_blocks[..., None] == jnp.arange(block_count, dtype=jnp.int32)).astype(
        jnp.float32
    )
    flipped_cols = psf_cols[:, ::-1]
    flipped_rows = psf_rows[:, ::-1]
    masks_for = jax.vmap(mask_of, in_axes=(None, None, 0, 0))

    def warp_and_blur(estimate_in):
        row_total = estimate_in.shape[0]
        blocks = estimate_in.reshape(row_total, block_count, 128)
        picked = blocks[:, warp_blocks]
        mapped = jnp.einsum("rvjki,vjkio->vrjo", picked, mats_full, precision=precise)
        mapped = mapped.reshape(visits_here, row_total, columns)
        return taps_along(pad_axis(mapped, 2, margin), psf_cols, 2, columns)

    col_width = columns // strips
    all_rows = rows_local * strips
    row_ids = jnp.arange(all_rows, dtype=jnp.int32)
    col_ids = strip_index * col_width + jnp.arange(col_width, dtype=jnp.int32)
    pixel_masks = masks_for(row_ids, col_ids, bad_boxes, footprints)
    observed = lax.all_to_all(exposures, "strip", split_axis=2, concat_axis=1, tiled=True).astype(
        jnp.float32
    )

    def model_image(image_in):
        transposed = lax.all_to_all(
            warp_and_blur(image_in), "strip", split_axis=2, concat_axis=1, tiled=True
        )
        return taps_along(pad_axis(transposed, 1, margin), psf_rows, 1, all_rows)

    residual = pixel_masks * model_image(sky_model) - pixel_masks * observed
    estimate = sky_model
    for step_index in range(STEPS):
        back_rows = taps_along(pad_axis(residual, 1, margin), flipped_rows, 1, all_rows)
        back_cols = taps_along(
            pad_axis(
                lax.all_to_all(back_rows, "strip", split_axis=1, concat_axis=2, tiled=True),
                2,
                margin,
            ),
            flipped_cols,
            2,
            columns,
        )
        unblur_blocks = back_cols.reshape(visits_here, rows_local, block_count, 128)
        spread = jnp.einsum("vrjo,vjkio->vrjki", unblur_blocks, mats_full, precision=precise)
        folded = jnp.einsum("vrjki,vjkb->rbi", spread, onehot, precision=precise)
        grad_part = folded.reshape(rows_local, columns)
        gradient = lax.psum(grad_part, "visit")
        image_grad = pixel_masks * model_image(gradient)
        grad_total, curvature = lax.psum(
            (jnp.sum(gradient * gradient) / visit_count, jnp.sum(image_grad * image_grad)),
            ("strip", "visit"),
        )
        step_size = grad_total / curvature
        estimate = estimate - step_size * gradient
        residual = residual - step_size * image_grad
    return estimate


def solution(mesh):
    return jax.shard_map(
        local,
        mesh=mesh,
        in_specs=(
            P("strip", None),
            P("visit", "strip", None),
            P("visit", None, None, None, None),
            P("visit", None, None),
            P("visit", None),
            P("visit", None),
            P("visit", None, None),
            P("visit", None),
        ),
        out_specs=P("strip", None),
        check_vma=False,
    )
```

profile of v0, /device:TPU:1, one launch (start us, length us, event | category | flops | bytes accessed | tf_op | source)
XLA Modules:
  0.0 885.4 jit_solution(17144647515702814789)
XLA Ops:
  20.3 9.5 %all-to-all-start.1 = ((bf16[32,2,8192]{2,1,0:T(2,128)(2,1)}), bf16[32,2,8192]{2,1,0:T(2,128)(2,1)}, u32[]{:S(2)}, u32[]{:S(2)}) async-start(bf16[32,2,8192]{2,1,0:T(2,128)(2,1)} %reshape.391), calls=%async_computation.1 | async-start | bytes 2097152 | tf_op jit(solution)/shard_map/all_to_all | solution.py:74
  34.9 10.3 %convolution_bitcast_fusion.4 = f32[4,32,4,8,128]{4,3,2,1,0:T(8,128)S(1)} fusion(f32[32,4,32,3,128]{4,0,3,2,1:T(8,128)} %bitcast.151, bf16[4,32,3,128,128]{4,3,2,1,0:T(8,128)(2,1)} %param.10), kind=kOutput, calls=%fused_computation.354 | convolution fusion | flops 2415919104 | bytes 20971520 | tf_op jit(solution)/shard_map/rvjki,vjkio->vrjo/dot_general | solution.py:65
  45.4 17.8 %multiply_add_fusion.6 = f32[4,32,4096]{2,1,0:T(8,128)S(1)} fusion(f32[4,32,4096]{2,1,0:T(8,128)S(1)} %bitcast.164, f32[4]{0:T(128)S(1)} %get-tuple-element.73, f32[4]{0:T(128)S(1)} %get-tuple-element.74, f32[4]{0:T(128)S(1)} %get-tuple-element.43, f32[4]{0:T(128)S(1)} %get-tuple-element.44, f32[4]{0:T(128)S(1)} %get-tuple-element.45, ...), kind=kLoop, calls=%fused_computation.318 | loop fusion | flops 34078720 | bytes 4194832 | tf_op jit(solution)/shard_map/add | solution.py:23
  69.1 8.7 reshape.393
  101.2 12.7 %all-to-all-done = f32[32,1,16384]{2,1,0:T(1,128)S(1)} async-done(((f32[32,1,16384]{2,1,0:T(1,128)}), f32[32,1,16384]{2,1,0:T(1,128)S(1)}, u32[]{:S(2)}, u32[]{:S(2)}) %all-to-all-start) | async-done | bytes 2097184 | tf_op jit(solution)/shard_map/all_to_all | solution.py:79
  129.4 7.9 copy.75
  137.3 39.9 %fusion.4 = (f32[4,1024,128]{2,1,0:T(8,128)S(1)}, pred[4,1024,128]{2,1,0:T(8,128)(4,1)}) fusion(f32[4,32,32,128]{3,1,2,0:T(8,128)S(1)} %copy-done.6, f32[4,1024,128]{2,1,0:T(8,128)} %bitcast.174, f32[4]{0:T(128)S(1)} %get-tuple-element.40, f32[4]{0:T(128)S(1)} %get-tuple-element.41, f32[4]{0:T(128)S(1)} %get-tuple-element.6, f32[4]{0:T(128)S(1)} %get-tuple-element.7, ...), kind=kOutput, calls=%fused_computation.15 | convolution fusion | flops 71745536 | bytes 6837264 | tf_op jit(solution)/shard_map/vmap()/dot_general | solution.py:34
  177.2 8.7 multiply_add_fusion.5
  187.3 32.8 %all_to_all.99 = f32[4,1024,128]{2,0,1:T(4,128)S(1)} all-to-all(f32[4,1024,128]{2,0,1:T(4,128)S(1)} %copy.48), channel_id=1, replica_groups=mesh['strip'=32,'visit'=4] {'strip'}, dimensions={1} | all-to-all | bytes 4194304 | tf_op jit(solution)/shard_map/all_to_all | solution.py:90
  222.9 42.3 %multiply_add_fusion.4 = f32[4,32,4096]{2,1,0:T(8,128)S(1)} fusion(f32[4,32,4096]{2,1,0:T(8,128)} %all_to_all.80, f32[4]{0:T(128)S(1)} %get-tuple-element.73, f32[4]{0:T(128)S(1)} %get-tuple-element.74, f32[4]{0:T(128)S(1)} %get-tuple-element.43, f32[4]{0:T(128)S(1)} %get-tuple-element.44, f32[4]{0:T(128)S(1)} %get-tuple-element.45, ...), kind=kLoop, calls=%fused_computation.220 | loop fusion | flops 34078720 | bytes 4194832 | tf_op jit(solution)/shard_map/add | solution.py:23
  265.7 16.6 %convolution_bitcast_fusion.1 = f32[4,32,32,3,128]{4,1,3,2,0:T(8,128)S(1)} fusion(bf16[4,32,3,128,128]{4,3,2,1,0:T(8,128)(2,1)} %param.10, f32[4,32,32,128,1]{3,2,1,0,4:T(8,128)S(1)} %bitcast_bitcast_fusion.1), kind=kOutput, calls=%fused_computation.8 | convolution fusion | flops 2415919104 | bytes 20971520 | tf_op jit(solution)/shard_map/vrjo,vjkio->vrjki/dot_general | solution.py:99
  289.5 39.8 %all-reduce.15.cloned.1.call-done = f32[32,4096]{1,0:T(8,128)} async-done(((f32[32,4096]{1,0:T(8,128)}), f32[32,4096]{1,0:T(8,128)}) %all-reduce.15.cloned.1.call-update) | async-done | bytes 524304 | tf_op jit(solution)/shard_map/psum | solution.py:102
  334.2 10.3 %convolution_bitcast_fusion.3 = f32[4,32,4,8,128]{4,3,2,1,0:T(8,128)S(1)} fusion(f32[32,4,32,3,128]{4,0,3,2,1:T(8,128)} %bitcast.152, bf16[4,32,3,128,128]{4,3,2,1,0:T(8,128)(2,1)} %param.10), kind=kOutput, calls=%fused_computation.353 | convolution fusion | flops 2415919104 | bytes 20971520 | tf_op jit(solution)/shard_map/rvjki,vjkio->vrjo/dot_general | solution.py:65
  344.7 18.0 %multiply_add_fusion.3 = f32[4,32,4096]{2,1,0:T(8,128)S(1)} fusion(f32[4,32,4096]{2,1,0:T(8,128)S(1)} %bitcast.169, f32[4]{0:T(128)S(1)} %get-tuple-element.73, f32[4]{0:T(128)S(1)} %get-tuple-element.74, f32[4]{0:T(128)S(1)} %get-tuple-element.43, f32[4]{0:T(128)S(1)} %get-tuple-element.44, f32[4]{0:T(128)S(1)} %get-tuple-element.45, ...), kind=kLoop, calls=%fused_computation.187 | loop fusion | flops 34078720 | bytes 4194832 | tf_op jit(solution)/shard_map/add | solution.py:23
  368.6 8.7 reshape.395
  377.3 9.9 %all-to-all-start.3 = ((f32[32,1,16384]{2,1,0:T(1,128)}), f32[32,1,16384]{2,1,0:T(1,128)}, u32[]{:S(2)}, u32[]{:S(2)}) async-start(f32[32,1,16384]{2,1,0:T(1,128)} %reshape.395), calls=%async_computation.3 | async-start | bytes 4194304 | tf_op jit(solution)/shard_map/all_to_all | solution.py:79
  388.8 27.1 %all-to-all-done.3 = f32[32,1,16384]{2,1,0:T(1,128)} async-done(((f32[32,1,16384]{2,1,0:T(1,128)}), f32[32,1,16384]{2,1,0:T(1,128)}, u32[]{:S(2)}, u32[]{:S(2)}) %all-to-all-start.3) | async-done | bytes 2097184 | tf_op jit(solution)/shard_map/all_to_all | solution.py:79
  429.5 7.8 copy.79
  437.3 39.7 %multiply_reduce_fusion.1 = (f32[]{:T(128)}, f32[4,1024,128]{2,1,0:T(8,128)S(1)}) fusion(f32[4]{0:T(128)S(1)} %get-tuple-element.5, f32[4]{0:T(128)S(1)} %get-tuple-element.40, f32[4]{0:T(128)S(1)} %get-tuple-element.41, f32[4]{0:T(128)S(1)} %get-tuple-element.6, f32[4]{0:T(128)S(1)} %get-tuple-element.7, f32[4]{0:T(128)S(1)} %get-tuple-element.8, ...), kind=kLoop, calls=%fused_computation.153 | loop fusion | flops 37224448 | bytes 4737556 | tf_op jit(solution)/shard_map/reduce_sum | solution.py:105
  477.0 64.3 %all-reduce.11 = (f32[]{:T(128)}, f32[]{:T(128)}) all-reduce(f32[]{:T(128)S(6)} %div.12, f32[]{:T(128)} %get-tuple-element.79), channel_id=1, replica_groups=mesh['strip'=32,'visit'=4] {'strip','visit'}, use_global_device_ids=true, to_apply=%region_2.3 | all-reduce | flops 2 | bytes 16 | tf_op jit(solution)/shard_map/psum | solution.py:104
  544.4 8.5 multiply_add_fusion.2
  554.3 32.8 %all_to_all.100 = f32[4,1024,128]{2,0,1:T(4,128)S(1)} all-to-all(f32[4,1024,128]{2,0,1:T(4,128)S(1)} %copy.57), channel_id=1, replica_groups=mesh['strip'=32,'visit'=4] {'strip'}, dimensions={1} | all-to-all | bytes 4194304 | tf_op jit(solution)/shard_map/all_to_all | solution.py:90
  589.9 42.3 %multiply_add_fusion.1 = f32[4,32,4096]{2,1,0:T(8,128)S(1)} fusion(f32[4,32,4096]{2,1,0:T(8,128)} %all_to_all.88, f32[4]{0:T(128)S(1)} %get-tuple-element.73, f32[4]{0:T(128)S(1)} %get-tuple-element.74, f32[4]{0:T(128)S(1)} %get-tuple-element.43, f32[4]{0:T(128)S(1)} %get-tuple-element.44, f32[4]{0:T(128)S(1)} %get-tuple-element.45, ...), kind=kLoop, calls=%fused_computation.86 | loop fusion | flops 34078720 | bytes 4194832 | tf_op jit(solution)/shard_map/add | solution.py:23
  632.7 16.3 %convolution_bitcast_fusion = f32[4,32,32,3,128]{4,1,3,2,0:T(8,128)S(1)} fusion(bf16[4,32,3,128,128]{4,3,2,1,0:T(8,128)(2,1)} %param.10, f32[4,32,32,128,1]{3,2,1,0,4:T(8,128)S(1)} %bitcast_bitcast_fusion), kind=kOutput, calls=%fused_computation.7 | convolution fusion | flops 2415919104 | bytes 20971520 | tf_op jit(solution)/shard_map/vrjo,vjkio->vrjki/dot_general | solution.py:99
  656.2 36.8 %all-reduce.17.cloned.1.call-done = f32[32,4096]{1,0:T(8,128)} async-done(((f32[32,4096]{1,0:T(8,128)}), f32[32,4096]{1,0:T(8,128)}) %all-reduce.17.cloned.1.call-update) | async-done | bytes 524304 | tf_op jit(solution)/shard_map/psum | solution.py:102
  698.0 10.3 %convolution_bitcast_fusion.2 = f32[4,32,4,8,128]{4,3,2,1,0:T(8,128)S(1)} fusion(f32[32,4,32,3,128]{4,0,3,2,1:T(8,128)} %bitcast.150, bf16[4,32,3,128,128]{4,3,2,1,0:T(8,128)(2,1)} %param.10), kind=kOutput, calls=%fused_computation.352 | convolution fusion | flops 2415919104 | bytes 20971520 | tf_op jit(solution)/shard_map/rvjki,vjkio->vrjo/dot_general | solution.py:65
  708.5 18.0 %multiply_add_fusion = f32[4,32,4096]{2,1,0:T(8,128)S(1)} fusion(f32[4,32,4096]{2,1,0:T(8,128)S(1)} %bitcast.163, f32[4]{0:T(128)S(1)} %get-tuple-element.73, f32[4]{0:T(128)S(1)} %get-tuple-element.74, f32[4]{0:T(128)S(1)} %get-tuple-element.43, f32[4]{0:T(128)S(1)} %get-tuple-element.44, f32[4]{0:T(128)S(1)} %get-tuple-element.45, ...), kind=kLoop, calls=%fused_computation.53 | loop fusion | flops 34078720 | bytes 4194832 | tf_op jit(solution)/shard_map/add | solution.py:23
  732.4 8.7 reshape.397
  741.1 10.4 %all-to-all-start.5 = ((f32[32,1,16384]{2,1,0:T(1,128)}), f32[32,1,16384]{2,1,0:T(1,128)}, u32[]{:S(2)}, u32[]{:S(2)}) async-start(f32[32,1,16384]{2,1,0:T(1,128)} %reshape.397), calls=%async_computation.5 | async-start | bytes 4194304 | tf_op jit(solution)/shard_map/all_to_all | solution.py:79
  752.9 27.0 %all-to-all-done.5 = f32[32,1,16384]{2,1,0:T(1,128)} async-done(((f32[32,1,16384]{2,1,0:T(1,128)}), f32[32,1,16384]{2,1,0:T(1,128)}, u32[]{:S(2)}, u32[]{:S(2)}) %all-to-all-start.5) | async-done | bytes 2097184 | tf_op jit(solution)/shard_map/all_to_all | solution.py:79
  800.0 11.1 %multiply_reduce_fusion = f32[]{:T(128)} fusion(f32[4,1024,128]{2,1,0:T(8,128)S(1)} %bitcast.162, pred[4,1024,128]{2,1,0:T(8,128)(4,1)} %get-tuple-element.86, f32[4]{0:T(128)S(1)} %get-tuple-element.40, f32[4]{0:T(128)S(1)} %get-tuple-element.41, f32[4]{0:T(128)S(1)} %get-tuple-element.6, f32[4]{0:T(128)S(1)} %get-tuple-element.7, ...), kind=kLoop, calls=%fused_computation.20 | loop fusion | flops 37224448 | bytes 2640404 | tf_op jit(solution)/shard_map/reduce_sum | solution.py:105
  811.1 63.9 %all-reduce.10 = (f32[]{:T(128)}, f32[]{:T(128)}) all-reduce(f32[]{:T(128)S(6)} %div.14, f32[]{:T(128)} %multiply_reduce_fusion), channel_id=1, replica_groups=mesh['strip'=32,'visit'=4] {'strip','visit'}, use_global_device_ids=true, to_apply=%region_7.8 | all-reduce | flops 2 | bytes 16 | tf_op jit(solution)/shard_map/psum | solution.py:104
  (85 shorter events, 148.8 us)
Async XLA Ops:
  20.3 9.5 %copy-start.4 = (f32[4,33]{1,0:T(4,128)S(1)}, f32[4,33]{1,0:T(4,128)}, u32[]{:S(2)}) copy-start(f32[4,33]{1,0:T(4,128)} %param.12) | copy-start | bytes 1588
  20.3 10.4 %copy-start.9 = (s32[4,32,3]{1,0,2:T(4,128)S(1)}, s32[4,32,3]{1,0,2:T(4,128)}, u32[]{:S(2)}) copy-start(s32[4,32,3]{1,0,2:T(4,128)} %param.11) | copy-start | bytes 4612
  20.3 10.8 %copy-start.8 = (f32[32,4096]{1,0:T(8,128)S(1)}, f32[32,4096]{1,0:T(8,128)}, u32[]{:S(2)}) copy-start(f32[32,4096]{1,0:T(8,128)} %param.8) | copy-start | bytes 1572868
  20.3 57.5 %all-to-all-start.1 = ((bf16[32,2,8192]{2,1,0:T(2,128)(2,1)}), bf16[32,2,8192]{2,1,0:T(2,128)(2,1)}, u32[]{:S(2)}, u32[]{:S(2)}) async-start(bf16[32,2,8192]{2,1,0:T(2,128)(2,1)} %reshape.391), calls=%async_computation.1 | async-start | bytes 2097152 | tf_op jit(solution)/shard_map/all_to_all | solution.py:74
  77.8 7.6 copy-start.10
  77.8 7.8 copy-start.5
  77.8 8.8 copy-start.11
  77.8 36.1 %all-to-all-start = ((f32[32,1,16384]{2,1,0:T(1,128)}), f32[32,1,16384]{2,1,0:T(1,128)S(1)}, u32[]{:S(2)}, u32[]{:S(2)}) async-start(f32[32,1,16384]{2,1,0:T(1,128)} %reshape.393), calls=%async_computation | async-start | bytes 4194304 | tf_op jit(solution)/shard_map/all_to_all | solution.py:79
  85.4 243.9 %all-reduce.15.cloned.1.call-start = ((), (), s32[]{:S(2)}) async-start(), calls=%async_computation.6 | async-start | bytes 1048576 | tf_op jit(solution)/shard_map/psum | solution.py:102
  114.0 1.4 copy-start.1
  129.4 7.9 copy-start.6
  177.2 8.7 copy-start
  377.3 10.2 %copy-start.2 = (f32[32,4096]{1,0:T(8,128)S(1)}, f32[32,4096]{1,0:T(8,128)}, u32[]{:S(2)}) copy-start(f32[32,4096]{1,0:T(8,128)} %all-reduce.15.cloned.1.call-done) | copy-start | bytes 1572868
  377.3 38.7 %all-to-all-start.3 = ((f32[32,1,16384]{2,1,0:T(1,128)}), f32[32,1,16384]{2,1,0:T(1,128)}, u32[]{:S(2)}, u32[]{:S(2)}) async-start(f32[32,1,16384]{2,1,0:T(1,128)} %reshape.395), calls=%async_computation.3 | async-start | bytes 4194304 | tf_op jit(solution)/shard_map/all_to_all | solution.py:79
  387.2 305.9 %all-reduce.17.cloned.1.call-start = ((), (), s32[]{:S(2)}) async-start(), calls=%async_computation.7 | async-start | bytes 1048576 | tf_op jit(solution)/shard_map/psum | solution.py:102
  429.5 7.8 copy-start.7
  741.1 10.4 %copy-start.3 = (f32[32,4096]{1,0:T(8,128)S(1)}, f32[32,4096]{1,0:T(8,128)}, u32[]{:S(2)}) copy-start(f32[32,4096]{1,0:T(8,128)} %all-reduce.17.cloned.1.call-done) | copy-start | bytes 1572868
  741.1 38.8 %all-to-all-start.5 = ((f32[32,1,16384]{2,1,0:T(1,128)}), f32[32,1,16384]{2,1,0:T(1,128)}, u32[]{:S(2)}, u32[]{:S(2)}) async-start(f32[32,1,16384]{2,1,0:T(1,128)} %reshape.397), calls=%async_computation.5 | async-start | bytes 4194304 | tf_op jit(solution)/shard_map/all_to_all | solution.py:79
Sparse Core Ops, SparseCore 0:
  289.6 39.6 all-reduce.14
  656.4 36.6 all-reduce.16
where the time goes:
time: 890 us; the launch traced here: 885 us
  other arithmetic  234 us (26%)
  blocking collectives  194 us (22%)
  local copies, waits for them, and re-layouts  143 us (16%)
  waiting for transfers between devices  143 us (16%)
  matrix products  116 us (13%)
  starting transfers between devices  37.6 us (4%)
  between operations  18.1 us (2%)
    add x7, other arithmetic, taps_along(): running = term if running is None else running + term  156 us
    psum x2, blocking collectives, local(): lax.psum((jnp.sum(gradient * gradient) / visit_count, jnp.sum(image_grad...  128 us
    psum x2, waiting for transfers between devices, local(): gradient = lax.psum(grad_part, 'visit')  76.6 us
    unnamed x37, local copies, waits for them, and re-layouts  69.6 us
    all_to_all x3, waiting for transfers between devices, model_image(): lax.all_to_all(warp_and_blur(image_in), 'strip', split_axis=2, concat_axi...  66.8 us
    all_to_all x2, blocking collectives, local(): lax.all_to_all(back_rows, 'strip', split_axis=1, concat_axis=2, tiled=True)  65.6 us
    reduce_sum x2, other arithmetic, local(): jnp.sum(image_grad * image_grad)  50.8 us
    dot_general x1, matrix products, mask_of(): covered = jnp.dot(row_hits.T, col_hits, preferred_element_type=jnp.float32)  39.9 us
  transfers between devices with their start and end apart: 6, of which 5 were waited for; matrix products, arithmetic and copies ran while one was open for 7% of the time, Pallas kernels for 0%

commit v1 on v0

v1 whole, which is shorter than its diff:
```python
import jax
import jax.numpy as jnp
from jax import lax
from jax.sharding import PartitionSpec as P

STEPS = 2

f32 = jnp.float32
bf16 = jnp.bfloat16


def split(a):
    hi = lax.reduce_precision(a, exponent_bits=8, mantissa_bits=7)
    return hi.astype(bf16), (a - hi).astype(bf16)


def mm(eq, a, b):
    return jnp.einsum(eq, a, b, preferred_element_type=f32)


def dot3(eq, a, b):
    a_hi, a_lo = split(a)
    b_hi, b_lo = split(b)
    return mm(eq, a_hi, b_hi) + (mm(eq, a_hi, b_lo) + mm(eq, a_lo, b_hi))


def dot2(eq, a, b_exact):
    a_hi, a_lo = split(a)
    return mm(eq, a_hi, b_exact) + mm(eq, a_lo, b_exact)


def mask_of(row_ids, col_ids, bad_list, footprint):
    row_hits = (
        (row_ids[None, :] >= bad_list[:, 0:1]) & (row_ids[None, :] < bad_list[:, 1:2])
    ).astype(f32)
    col_hits = (
        (col_ids[None, :] >= bad_list[:, 2:3]) & (col_ids[None, :] < bad_list[:, 3:4])
    ).astype(f32)
    covered = jnp.dot(row_hits.T, col_hits, preferred_element_type=f32)
    inside_rows = ((row_ids >= footprint[0]) & (row_ids < footprint[1])).astype(f32)
    inside_cols = ((col_ids >= footprint[2]) & (col_ids < footprint[3])).astype(f32)
    return (
        jnp.where(covered > 0.5, 0.0, 1.0).astype(f32)
        * inside_rows[:, None]
        * inside_cols[None, :]
    )


def local(sky_model, exposures, warp_mats, warp_blocks, psf_cols, psf_rows, bad_boxes, footprints):
    strips = lax.axis_size("strip")
    strip_index = lax.axis_index("strip")
    rows = sky_model.shape[0]
    columns = sky_model.shape[1]
    nb = columns // 128
    visits_here = warp_mats.shape[0]
    taps = psf_cols.shape[1]
    margin = taps // 2
    ext = rows + 2 * margin

    r_id = jnp.arange(rows)[:, None]
    e_id = jnp.arange(ext)[None, :]
    t_id = e_id - r_id
    row_band = jnp.where(
        (t_id >= 0) & (t_id < taps), psf_rows[:, jnp.clip(t_id, 0, taps - 1)], 0.0
    )

    d_id = jnp.arange(3)[:, None, None] - 1
    i_id = jnp.arange(128)[None, :, None]
    o_id = jnp.arange(128)[None, None, :]
    c_t = 128 * d_id + i_id - o_id + margin
    col_band = jnp.where(
        (c_t >= 0) & (c_t < taps), psf_cols[:, jnp.clip(c_t, 0, taps - 1)], 0.0
    )
    col_band_t = jnp.swapaxes(col_band, 2, 3)

    onehot = (warp_blocks[..., None] == jnp.arange(nb, dtype=jnp.int32)).astype(bf16)

    row_ids = strip_index * rows + jnp.arange(rows, dtype=jnp.int32)
    col_ids = jnp.arange(columns, dtype=jnp.int32)
    pixel_masks = jax.vmap(mask_of, in_axes=(None, None, 0, 0))(
        row_ids, col_ids, bad_boxes, footprints
    )

    up = [(s, s - 1) for s in range(1, strips)]
    down = [(s, s + 1) for s in range(strips - 1)]

    def with_halo(x):
        above = lax.ppermute(x[rows - margin:], "strip", down)
        below = lax.ppermute(x[:margin], "strip", up)
        return jnp.concatenate([above, x, below], axis=0)

    def shift_blocks(y, d):
        if d == 0:
            return y
        zeros = jnp.zeros_like(y[..., :1, :])
        if d > 0:
            return jnp.concatenate([y[..., d:, :], zeros], axis=-2)
        return jnp.concatenate([zeros, y[..., :d, :]], axis=-2)

    def forward(x_ext):
        blurred_rows = dot3("vre,ec->vrc", row_band, x_ext)
        hi, lo = split(blurred_rows)
        hi = hi.reshape(visits_here, rows, nb, 128)
        lo = lo.reshape(visits_here, rows, nb, 128)
        pick = jax.vmap(lambda u, wb: u[:, wb])
        warped = mm("vrjki,vjkio->vrjo", pick(hi, warp_blocks), warp_mats) + mm(
            "vrjki,vjkio->vrjo", pick(lo, warp_blocks), warp_mats
        )
        out = None
        for d in range(3):
            term = dot3("vrji,vio->vrjo", shift_blocks(warped, d - 1), col_band[:, d])
            out = term if out is None else out + term
        return pixel_masks * out.reshape(visits_here, rows, columns)

    def adjoint_partial(res):
        z = res.reshape(visits_here, rows, nb, 128)
        back = None
        for d in range(3):
            term = dot3("vrji,vio->vrjo", shift_blocks(z, 1 - d), col_band_t[:, d])
            back = term if back is None else back + term
        spread = dot2("vrjo,vjkio->vrjki", back, warp_mats)
        folded = dot2("vrjki,vjkb->vrbi", spread, onehot)
        folded = folded.reshape(visits_here, rows, columns)
        return dot3("vre,vrc->ec", row_band, folded)

    def reduce_partial(part):
        from_below = lax.ppermute(part[ext - margin:], "strip", down)
        from_above = lax.ppermute(part[:margin], "strip", up)
        mid = part[margin:margin + rows]
        mid = mid + jnp.concatenate(
            [from_below, jnp.zeros((rows - margin, columns), f32)], axis=0
        )
        mid = mid + jnp.concatenate(
            [jnp.zeros((rows - margin, columns), f32), from_above], axis=0
        )
        return lax.psum(mid, "visit")

    observed = exposures.astype(f32)
    estimate = sky_model
    residual = forward(with_halo(sky_model)) - pixel_masks * observed
    for step_index in range(STEPS):
        gradient = reduce_partial(adjoint_partial(residual))
        image_grad = forward(with_halo(gradient))
        grad_total, curvature = lax.psum(
            (jnp.sum(gradient * gradient) / lax.axis_size("visit"), jnp.sum(image_grad * image_grad)),
            ("strip", "visit"),
        )
        step_size = grad_total / curvature
        estimate = estimate - step_size * gradient
        residual = residual - step_size * image_grad
    return estimate


def solution(mesh):
    return jax.shard_map(
        local,
        mesh=mesh,
        in_specs=(
            P("strip", None),
            P("visit", "strip", None),
            P("visit", None, None, None, None),
            P("visit", None, None),
            P("visit", None),
            P("visit", None),
            P("visit", None, None),
            P("visit", None),
        ),
        out_specs=P("strip", None),
        check_vma=False,
    )
```

time: 890 us -> 724 us (0.81)
  other arithmetic: 234 us -> 20.3 us
  local copies, waits for them, and re-layouts: 143 us -> 259 us
  blocking collectives: 194 us -> 133 us
  waiting for transfers between devices: 143 us -> 103 us
  matrix products: 116 us -> 147 us
    gather x3 -> x13, local copies, waits for them, and re-layouts: 11.5 us -> 228 us  [the longest x3 195 us: local(): psf_cols[:, jnp.clip(c_t, 0, taps - 1)]]
    add x8 -> x4, other arithmetic: 156 us -> 1.77 us  [the longest x2 1.69 us: reduce_partial(): mid + jnp.concatenate([jnp.zeros((rows - margin, columns), f32), from_abo...]
    all_to_all x4 -> x0, waiting for transfers between devices: 66.8 us -> none  [the longest x3 66.8 us: model_image(): lax.all_to_all(warp_and_blur(image_in), 'strip', split_axis=2, concat_axi...]
    all_to_all x2 -> x0, blocking collectives: 65.6 us -> none  [local(): lax.all_to_all(back_rows, 'strip', split_axis=1, concat_axis=2, tiled=True)]
    unnamed x37 -> x91, local copies, waits for them, and re-layouts: 69.6 us -> 10.4 us
    reduce_sum x2, other arithmetic: 50.8 us -> 7 us  [local(): jnp.sum(image_grad * image_grad)]
    all_to_all x4 -> x0, starting transfers between devices: 37.3 us -> none  [the longest x3 27.8 us: model_image(): lax.all_to_all(warp_and_blur(image_in), 'strip', split_axis=2, concat_axi...]
    ppermute x0 -> x10, starting transfers between devices: none -> 33.1 us  [the longest x3 16.2 us: with_halo(): above = lax.ppermute(x[rows - margin:], 'strip', down)]
  transfers between devices with their start and end apart: 6 -> 12, of which waited for: 5 -> 10; matrix products, arithmetic and copies ran while one was open for 7% -> 29% of each run, Pallas kernels for 0% -> 0%
where the time goes in v1:
time: 724 us; the launch traced here: 714 us
  local copies, waits for them, and re-layouts  259 us (36%)
  matrix products  147 us (20%)
  blocking collectives  133 us (18%)
  waiting for transfers between devices  103 us (14%)
  starting transfers between devices  33.1 us (5%)
  other arithmetic  20.3 us (3%)
  between operations  18.7 us (3%)
    gather x3, local copies, waits for them, and re-layouts, local(): psf_cols[:, jnp.clip(c_t, 0, taps - 1)]  195 us
    dot_general x74, matrix products, mm(): return jnp.einsum(eq, a, b, preferred_element_type=f32)  144 us
    psum x2, blocking collectives, local(): lax.psum((jnp.sum(gradient * gradient) / lax.axis_size('visit'), jnp.sum(...  133 us
    psum x2, waiting for transfers between devices, reduce_partial(): return lax.psum(mid, 'visit')  88.3 us
    gather x8, local copies, waits for them, and re-layouts, forward(): pick = jax.vmap(lambda u, wb: u[:, wb])  26.4 us
    ppermute x3, starting transfers between devices, with_halo(): above = lax.ppermute(x[rows - margin:], 'strip', down)  16.2 us
  transfers between devices with their start and end apart: 12, of which 10 were waited for; matrix products, arithmetic and copies ran while one was open for 29% of the time, Pallas kernels for 0%

profile of v1, /device:TPU:1, one launch (start us, length us, event | category | flops | bytes accessed | tf_op | source)
XLA Modules:
  0.0 714.3 jit_solution(16506754345738003485)
XLA Ops:
  8.4 4.5 collective-permute-start
  16.1 163.1 %gather_fusion.1 = f32[49152,4]{1,0:T(8,128)} fusion(f32[4,33]{0,1:T(8,128)S(1)} %copy.79, s32[49152]{0:T(1024)S(1)} %broadcast_clamp_fusion), kind=kCustom, calls=%fused_computation.1 | custom fusion | bytes 1769472 | tf_op jit(solution)/shard_map/gather | solution.py:72
  179.1 17.7 %copy.91 = f32[3,128,128,4]{1,2,3,0:T(8,128)S(1)} copy(f32[3,128,128,4]{3,2,1,0:T(8,128)} %bitcast.442) | data formatting | bytes 1572864 | tf_op jit(solution)/shard_map/gather | solution.py:72
  196.8 14.8 %copy.81 = f32[3,128,128,4]{2,1,3,0:T(8,128)S(1)} copy(f32[3,128,128,4]{3,2,1,0:T(8,128)} %bitcast.443) | data formatting | bytes 1572864 | tf_op jit(solution)/shard_map/gather | solution.py:72
  211.8 5.5 gather_fusion
  224.8 4.3 gather_fusion.3
  229.2 4.4 gather_fusion.2
  233.5 8.0 %fusion.271 = f32[4,32,32,128,1]{3,2,4,1,0:T(8,128)S(1)} fusion(bf16[4,32,32,3,128]{4,1,3,2,0:T(8,128)(2,1)} %bitcast.461, bf16[4,32,3,128,128]{4,3,2,1,0:T(8,128)(2,1)} %param.10), kind=kOutput, calls=%fused_computation.372 | convolution fusion | flops 402653184 | bytes 17825792 | tf_op jit(solution)/shard_map/vrjki,vjkio->vrjo/dot_general | solution.py:18
  241.5 6.1 fusion.19
  258.3 3.8 multiply_subtract_fusion.1
  271.3 11.7 %fusion.79 = f32[4,32,32,3,128]{4,2,3,1,0:T(8,128)} fusion(bf16[4,32,3,128,128]{4,3,2,1,0:T(8,128)(2,1)} %param.10, bf16[4,32,32,128,1]{3,2,1,0,4:T(8,128)(2,1)S(1)} %get-tuple-element.35), kind=kOutput, calls=%fused_computation.163 | convolution fusion | flops 402653184 | bytes 19922944 | tf_op jit(solution)/shard_map/vrjo,vjkio->vrjki/dot_general | solution.py:18
  283.1 13.0 %reduce-precision_convert_fusion.1 = (bf16[4,32,32,3,128]{4,1,3,2,0:T(8,128)(2,1)S(1)}, bf16[4,32,32,3,128]{4,1,3,2,0:T(8,128)(2,1)}) fusion(f32[4,32,32,3,128]{4,2,3,1,0:T(8,128)} %fusion.79, bf16[4,32,3,128,128]{4,3,2,1,0:T(8,128)(2,1)} %param.10, bf16[4,32,32,128,1]{3,2,1,0,4:T(8,128)(2,1)} %get-tuple-element.36), kind=kOutput, calls=%fused_computation.11 | convolution fusion | flops 410517504 | bytes 26214400 | tf_op jit(solution)/shard_map/vrjo,vjkio->vrjki/dot_general | solution.py:18
  307.8 3.6 collective-permute-start.2
  315.7 46.1 %all-reduce.19.cloned.1.call-done = f32[32,4096]{1,0:T(8,128)} async-done(((f32[32,4096]{1,0:T(8,128)}), f32[32,4096]{1,0:T(8,128)}) %all-reduce.19.cloned.1.call-update) | async-done | bytes 524304 | tf_op jit(solution)/shard_map/psum | solution.py:136
  362.9 5.9 collective-permute-start.4
  378.1 4.3 gather_fusion.5
  382.6 4.4 gather_fusion.4
  387.0 8.0 %fusion.272 = f32[4,32,32,128,1]{3,2,4,1,0:T(8,128)S(1)} fusion(bf16[4,32,32,3,128]{4,1,3,2,0:T(8,128)(2,1)} %bitcast.462, bf16[4,32,3,128,128]{4,3,2,1,0:T(8,128)(2,1)} %param.10), kind=kOutput, calls=%fused_computation.373 | convolution fusion | flops 402653184 | bytes 17825792 | tf_op jit(solution)/shard_map/vrjki,vjkio->vrjo/dot_general | solution.py:18
  395.0 5.9 fusion.28
  406.6 3.2 add_add_fusion.2
  412.7 4.1 multiply_reduce_fusion.1
  417.4 66.6 %all-reduce.15 = (f32[]{:T(128)}, f32[]{:T(128)}) all-reduce(f32[]{:T(128)S(6)} %div.12, f32[]{:T(128)} %get-tuple-element.13), channel_id=1, replica_groups=mesh['strip'=32,'visit'=4] {'strip','visit'}, use_global_device_ids=true, to_apply=%region_2.3 | all-reduce | flops 2 | bytes 16 | tf_op jit(solution)/shard_map/psum | solution.py:144
  496.6 11.7 %fusion.75 = f32[4,32,32,3,128]{4,2,3,1,0:T(8,128)} fusion(bf16[4,32,3,128,128]{4,3,2,1,0:T(8,128)(2,1)} %param.10, bf16[4,32,32,128,1]{3,2,1,0,4:T(8,128)(2,1)S(1)} %get-tuple-element.25), kind=kOutput, calls=%fused_computation.159 | convolution fusion | flops 402653184 | bytes 19922944 | tf_op jit(solution)/shard_map/vrjo,vjkio->vrjki/dot_general | solution.py:18
  508.4 13.0 %reduce-precision_convert_fusion = (bf16[4,32,32,3,128]{4,1,3,2,0:T(8,128)(2,1)S(1)}, bf16[4,32,32,3,128]{4,1,3,2,0:T(8,128)(2,1)}) fusion(f32[4,32,32,3,128]{4,2,3,1,0:T(8,128)} %fusion.75, bf16[4,32,3,128,128]{4,3,2,1,0:T(8,128)(2,1)} %param.10, bf16[4,32,32,128,1]{3,2,1,0,4:T(8,128)(2,1)} %get-tuple-element.26), kind=kOutput, calls=%fused_computation.9 | convolution fusion | flops 410517504 | bytes 26214400 | tf_op jit(solution)/shard_map/vrjo,vjkio->vrjki/dot_general | solution.py:18
  540.9 42.2 %all-reduce.21.cloned.1.call-done = f32[32,4096]{1,0:T(8,128)} async-done(((f32[32,4096]{1,0:T(8,128)}), f32[32,4096]{1,0:T(8,128)}) %all-reduce.21.cloned.1.call-update) | async-done | bytes 524304 | tf_op jit(solution)/shard_map/psum | solution.py:136
  584.3 5.9 collective-permute-start.8
  599.5 4.3 gather_fusion.7
  604.0 4.4 gather_fusion.6
  608.4 8.0 %fusion.273 = f32[4,32,32,128,1]{3,2,4,1,0:T(8,128)S(1)} fusion(bf16[4,32,32,3,128]{4,1,3,2,0:T(8,128)(2,1)} %bitcast.460, bf16[4,32,3,128,128]{4,3,2,1,0:T(8,128)(2,1)} %param.10), kind=kOutput, calls=%fused_computation.374 | convolution fusion | flops 402653184 | bytes 17825792 | tf_op jit(solution)/shard_map/vrjki,vjkio->vrjo/dot_general | solution.py:18
  616.4 5.9 fusion.37
  628.0 3.2 add_add_fusion
  637.6 66.3 %all-reduce.14 = (f32[]{:T(128)}, f32[]{:T(128)}) all-reduce(f32[]{:T(128)S(6)} %div.14, f32[]{:T(128)} %multiply_reduce_fusion), channel_id=1, replica_groups=mesh['strip'=32,'visit'=4] {'strip','visit'}, use_global_device_ids=true, to_apply=%region_7.8 | all-reduce | flops 2 | bytes 16 | tf_op jit(solution)/shard_map/psum | solution.py:144
  (232 shorter events, 121.9 us)
Async XLA Ops:
  6.5 355.2 %all-reduce.19.cloned.1.call-start = ((), (), s32[]{:S(2)}) async-start(), calls=%async_computation | async-start | bytes 1048576 | tf_op jit(solution)/shard_map/psum | solution.py:136
  8.4 212.6 %collective-permute-start = (f32[16,4096]{1,0:T(8,128)}, f32[16,4096]{1,0:T(8,128)}, u32[]{:S(2)}, u32[]{:S(2)}) collective-permute-start(f32[16,4096]{1,0:T(8,128)} %get-tuple-element.76), channel_id=1, source_target_pairs={{0,4},{4,8},{8,12},{12,16},{16,20},{20,24},{24,28},{28,32},{32,36}... | collective-permute-start | bytes 786440 | tf_op jit(solution)/shard_map/ppermute | solution.py:88
  12.9 209.1 %collective-permute-start.1 = (f32[16,4096]{1,0:T(8,128)}, f32[16,4096]{1,0:T(8,128)}, u32[]{:S(2)}, u32[]{:S(2)}) collective-permute-start(f32[16,4096]{1,0:T(8,128)} %get-tuple-element.75), channel_id=1, source_target_pairs={{4,0},{8,4},{12,8},{16,12},{20,16},{24,20},{28,24},{32,28},{36,32}... | collective-permute-start | bytes 786440 | tf_op jit(solution)/shard_map/ppermute | solution.py:89
  196.8 14.8 %copy-start.40 = (f32[4,33]{1,0:T(4,128)S(1)}, f32[4,33]{1,0:T(4,128)}, u32[]{:S(2)}) copy-start(f32[4,33]{1,0:T(4,128)} %param.13) | copy-start | bytes 1588
  217.3 2.4 copy-start.37
  219.4 49.6 %copy-start.20 = (bf16[4,128,128,1]{2,1,3,0:T(8,128)(2,1)}, bf16[4,128,128,1]{2,1,3,0:T(8,128)(2,1)S(1)}, u32[]{:S(2)}) copy-start(bf16[4,128,128,1]{2,1,3,0:T(8,128)(2,1)S(1)} %get-tuple-element.62) | copy-start | bytes 393220
  219.4 2.5 copy-start.12
  220.3 2.7 copy-start.26
  220.3 3.5 copy-start.15
  220.4 31.0 %copy-start = (f32[4,3,128,128]{3,2,0,1:T(8,128)}, f32[4,3,128,128]{3,2,0,1:T(8,128)S(1)}, u32[]{:S(2)}) copy-start(f32[4,3,128,128]{3,2,0,1:T(8,128)S(1)} %select_bitcast_fusion) | copy-start | bytes 2359300
  233.5 8.0 %copy-start.8 = (bf16[384,32,128]{2,1,0:T(8,128)(2,1)S(1)}, bf16[384,32,128]{2,1,0:T(8,128)(2,1)}, u32[]{:S(2)}) copy-start(bf16[384,32,128]{2,1,0:T(8,128)(2,1)} %gather_fusion.3) | copy-start | bytes 9437188
  256.1 2.2 copy-start.36
  256.1 2.2 copy-start.39
  305.9 7.7 %collective-permute-start.3 = (f32[16,4096]{1,0:T(8,128)S(1)}, f32[16,4096]{1,0:T(8,128)S(1)}, u32[]{:S(2)}, u32[]{:S(2)}) collective-permute-start(f32[16,4096]{1,0:T(8,128)S(1)} %get-tuple-element.60), channel_id=1, source_target_pairs={{4,0},{8,4},{12,8},{16,12},{20,16},{24,20},{28,24},{32,28},{36,32}... | collective-permute-start | bytes 786440 | tf_op jit(solution)/shard_map/ppermute | solution.py:128
  307.8 6.9 collective-permute-start.2
  315.6 60.8 %copy-start.28 = (bf16[4,32,64]{2,1,0:T(8,128)(2,1)S(1)}, bf16[4,32,64]{2,1,0:T(8,128)(2,1)}, u32[]{:S(2)}) copy-start(bf16[4,32,64]{2,1,0:T(8,128)(2,1)} %copy-done.26) | copy-start | bytes 49156
  315.6 267.5 %all-reduce.21.cloned.1.call-start = ((), (), s32[]{:S(2)}) async-start(), calls=%async_computation.1 | async-start | bytes 1048576 | tf_op jit(solution)/shard_map/psum | solution.py:136
  362.9 9.2 %collective-permute-start.4 = (f32[16,4096]{1,0:T(8,128)S(1)}, f32[16,4096]{1,0:T(8,128)S(1)}, u32[]{:S(2)}, u32[]{:S(2)}) collective-permute-start(f32[16,4096]{1,0:T(8,128)S(1)} %get-tuple-element.74), channel_id=1, source_target_pairs={{0,4},{4,8},{8,12},{12,16},{16,20},{20,24},{24,28},{28,32},{32,36}... | collective-permute-start | bytes 786440 | tf_op jit(solution)/shard_map/ppermute | solution.py:88
  368.7 7.7 %collective-permute-start.5 = (f32[16,4096]{1,0:T(8,128)S(1)}, f32[16,4096]{1,0:T(8,128)S(1)}, u32[]{:S(2)}, u32[]{:S(2)}) collective-permute-start(f32[16,4096]{1,0:T(8,128)S(1)} %get-tuple-element.73), channel_id=1, source_target_pairs={{4,0},{8,4},{12,8},{16,12},{20,16},{24,20},{28,24},{32,28},{36,32}... | collective-permute-start | bytes 786440 | tf_op jit(solution)/shard_map/ppermute | solution.py:89
  373.8 3.0 copy-start.17
  387.0 8.0 %copy-start.7 = (bf16[384,32,128]{2,1,0:T(8,128)(2,1)S(1)}, bf16[384,32,128]{2,1,0:T(8,128)(2,1)}, u32[]{:S(2)}) copy-start(bf16[384,32,128]{2,1,0:T(8,128)(2,1)} %gather_fusion.5) | copy-start | bytes 9437188
  409.8 2.9 copy-start.3
  531.2 7.7 %collective-permute-start.7 = (f32[16,4096]{1,0:T(8,128)S(1)}, f32[16,4096]{1,0:T(8,128)S(1)}, u32[]{:S(2)}, u32[]{:S(2)}) collective-permute-start(f32[16,4096]{1,0:T(8,128)S(1)} %get-tuple-element.58), channel_id=1, source_target_pairs={{4,0},{8,4},{12,8},{16,12},{20,16},{24,20},{28,24},{32,28},{36,32}... | collective-permute-start | bytes 786440 | tf_op jit(solution)/shard_map/ppermute | solution.py:128
  533.7 6.3 collective-permute-start.6
  540.9 56.9 %copy-start.30 = (bf16[4,32,64]{2,1,0:T(8,128)(2,1)S(1)}, bf16[4,32,64]{2,1,0:T(8,128)(2,1)}, u32[]{:S(2)}) copy-start(bf16[4,32,64]{2,1,0:T(8,128)(2,1)} %copy-done.26) | copy-start | bytes 49156
  584.3 9.2 %collective-permute-start.8 = (f32[16,4096]{1,0:T(8,128)S(1)}, f32[16,4096]{1,0:T(8,128)S(1)}, u32[]{:S(2)}, u32[]{:S(2)}) collective-permute-start(f32[16,4096]{1,0:T(8,128)S(1)} %get-tuple-element.68), channel_id=1, source_target_pairs={{0,4},{4,8},{8,12},{12,16},{16,20},{20,24},{24,28},{28,32},{32,36}... | collective-permute-start | bytes 786440 | tf_op jit(solution)/shard_map/ppermute | solution.py:88
  590.1 7.7 %collective-permute-start.9 = (f32[16,4096]{1,0:T(8,128)S(1)}, f32[16,4096]{1,0:T(8,128)S(1)}, u32[]{:S(2)}, u32[]{:S(2)}) collective-permute-start(f32[16,4096]{1,0:T(8,128)S(1)} %get-tuple-element.67), channel_id=1, source_target_pairs={{4,0},{8,4},{12,8},{16,12},{20,16},{24,20},{28,24},{32,28},{36,32}... | collective-permute-start | bytes 786440 | tf_op jit(solution)/shard_map/ppermute | solution.py:89
  595.2 3.0 copy-start.19
  608.4 8.0 %copy-start.6 = (bf16[384,32,128]{2,1,0:T(8,128)(2,1)S(1)}, bf16[384,32,128]{2,1,0:T(8,128)(2,1)}, u32[]{:S(2)}) copy-start(bf16[384,32,128]{2,1,0:T(8,128)(2,1)} %gather_fusion.7) | copy-start | bytes 9437188
  631.2 2.9 copy-start.4
  634.1 71.2 %copy-start.13 = (f32[32,4096]{1,0:T(8,128)S(1)}, f32[32,4096]{1,0:T(8,128)}, u32[]{:S(2)}) copy-start(f32[32,4096]{1,0:T(8,128)} %param.8) | copy-start | bytes 1572868
  634.1 71.2 %copy-start.14 = (f32[32,4096]{1,0:T(8,128)S(1)}, f32[32,4096]{1,0:T(8,128)}, u32[]{:S(2)}) copy-start(f32[32,4096]{1,0:T(8,128)} %all-reduce.19.cloned.1.call-done) | copy-start | bytes 1572868
  (21 other events, 27.1 us)
Sparse Core Ops, SparseCore 0:
  315.8 45.9 all-reduce.18
  541.1 42.0 all-reduce.20
